TPU v7x, 128 devices: a whole 4x4x4 slice. The times are simulated.
128 devices in a mesh: grp: 8 (over x_hi, z), vocab: 16 (over y, x_lo, core).
Axes of the slice: x: 4 (x_hi: 2, x_lo: 2; x = x_hi * 2 + x_lo), y: 4, z: 4, core: 2. Of those that a mesh axis runs over, the one named last changes fastest.
Arguments:
- hidden: bfloat16 [1024, 8192], P('grp', 'vocab')
- head_weight: bfloat16 [81920, 8192], P(('grp', 'vocab'))
- targets: int32 [1024], replicated, may hold values from 0 to 81919
- old_logprobs: float32 [1024], replicated
- loss_mask: int32 [1024], replicated, may hold values 0 or 1
- beam_lengths: int32 [128], replicated, may hold values from 1 to 24, 1024 in all
- beam_group: int32 [128], replicated, may hold values from 0 to 1, as said below
- rewards: float32 [128], replicated, may hold values from 0 to 1, as said below
Outputs:
- logprob: float32 [1024], replicated
- total_loss: float32 [], replicated
- head_grad: bfloat16 [81920, 8192], P(('grp', 'vocab'))
Inputs may be any that keep to these rules, and one draw needn't show every extreme that they name: `beam_group`: each of the 2 groups is named by exactly 64 beams. `rewards`: multiples of 1/8.
All inputs are finite; a program needn't handle non-finite values.
Results may differ from a plain program's by a relative error of at most 0.005.
Values may be sent and summed in bfloat16 or wider, within the bound.
No kernel may reach another device: no remote copies, remote signals or barrier semaphores. Data moves between devices by JAX's collectives and lax.ppermute only.
A program may use at most 128 MiB of HBM per device.

v0:
```python
import jax
import jax.numpy as jnp
from jax import lax
from jax.sharding import PartitionSpec as P

GROUP_BEAMS = 64


def policy_terms(logprob, old_logprobs, loss_mask, beam_lengths, beam_group, rewards):
    highest = lax.Precision.HIGHEST
    tok_count = logprob.shape[0]
    beam_count = beam_lengths.shape[0]
    group_count = beam_count // GROUP_BEAMS
    beam_ends = jnp.cumsum(beam_lengths)
    position = jnp.arange(tok_count, dtype=jnp.int32)
    beam_of = jnp.sum((position[:, None] >= beam_ends[None, :]).astype(jnp.int32), axis=1)
    token_beam = (beam_of[:, None] == jnp.arange(beam_count, dtype=jnp.int32)[None, :]).astype(
        jnp.float32
    )
    beam_onehot = (beam_group[:, None] == jnp.arange(group_count, dtype=jnp.int32)[None, :]).astype(
        jnp.float32
    )
    group_mean = jnp.dot(rewards, beam_onehot, precision=highest) / GROUP_BEAMS
    centred = rewards - jnp.dot(beam_onehot, group_mean, precision=highest)
    group_var = jnp.dot(centred * centred, beam_onehot, precision=highest) / GROUP_BEAMS
    advantage = centred / jnp.sqrt(jnp.dot(beam_onehot, group_var, precision=highest) + 1e-06)
    weight = loss_mask.astype(jnp.float32)
    counts = jnp.dot(weight, token_beam, precision=highest)
    token_adv = jnp.dot(token_beam, advantage, precision=highest)
    token_norm = jnp.dot(token_beam, jnp.maximum(counts, 1.0), precision=highest)
    ratios = jnp.exp(logprob - old_logprobs)
    clipped = jnp.clip(ratios, 0.8, 1.2)
    plain_term = ratios * token_adv
    bounded = clipped * token_adv
    token_share = weight / token_norm
    total_loss = -jnp.sum(token_share * jnp.minimum(plain_term, bounded))
    slopes = -token_share * jnp.where(plain_term <= bounded, plain_term, 0.0)
    return (total_loss, slopes)


def shards(
    hidden, head_weight, targets, old_logprobs, loss_mask, beam_lengths, beam_group, rewards
):
    token_block = lax.all_gather(hidden, "grp", axis=0, tiled=True)
    features = lax.all_gather(token_block, "vocab", axis=1, tiled=True)
    shard = head_weight.shape[0]
    offset = (lax.axis_index("grp") * lax.axis_size("vocab") + lax.axis_index("vocab")) * shard
    vocab_ids = offset + jnp.arange(shard, dtype=jnp.int32)
    logits = lax.dot_general(
        features, head_weight, (((1,), (1,)), ((), ())), preferred_element_type=jnp.float32
    )
    hits = targets[:, None] == vocab_ids[None, :]
    picked = jnp.sum(jnp.where(hits, logits, 0.0), axis=1)
    top = lax.pmax(jnp.max(logits, axis=1), ("grp", "vocab"))
    local_sum = jnp.sum(jnp.exp(logits - top[:, None]), axis=1)
    total, target_logit = lax.psum((local_sum, picked), ("grp", "vocab"))
    log_total = top + jnp.log(total)
    logprob = target_logit - log_total
    total_loss, slopes = policy_terms(
        logprob, old_logprobs, loss_mask, beam_lengths, beam_group, rewards
    )
    grads = (
        slopes[:, None] * (hits.astype(jnp.float32) - jnp.exp(logits - log_total[:, None]))
    ).astype(jnp.bfloat16)
    head_grad = lax.dot_general(
        grads, features, (((0,), (0,)), ((), ())), preferred_element_type=jnp.float32
    )
    return (logprob, total_loss, head_grad.astype(jnp.bfloat16))


def solution(mesh):
    in_specs = (P("grp", "vocab"), P(("grp", "vocab"), None), P(), P(), P(), P(), P(), P())
    out_specs = (P(), P(), P(("grp", "vocab"), None))
    return jax.shard_map(shards, mesh=mesh, in_specs=in_specs, out_specs=out_specs, check_vma=False)
```

profile of v0, /device:TPU:1, one launch (start us, length us, event | category | flops | bytes accessed | tf_op | source)
XLA Modules:
  0.0 327.0 jit_solution(1257413996547602422)
XLA Ops:
  7.2 0.0 all-gather.3.cloned.1.call-start
  7.2 0.7 all-gather.3.cloned.1.call-update
  7.9 0.0 all-gather.5.cloned.1.call-start
  7.9 50.5 %all-gather.3.cloned.1.call-done = bf16[1024,512]{1,0:T(8,128)(2,1)} async-done(((bf16[128,512]{1,0:T(8,128)(2,1)}), bf16[1024,512]{1,0:T(8,128)(2,1)}) %all-gather.3.cloned.1.call-update) | async-done | bytes 1048592 | tf_op jit(solution)/shard_map/all_gather | solution.py:44
  58.4 0.0 all-gather.5.cloned.1.call-update
  58.4 0.7 convert_element_type.17
  59.1 0.8 copy.13
  59.9 0.2 reduce-window.8
  60.1 0.1 reduce
  60.2 0.9 fusion.15
  61.0 0.9 fusion.13
  61.9 0.9 fusion.12
  62.9 0.9 fusion.17
  63.7 0.3 convert_reduce_fusion
  64.0 0.4 fusion.19
  64.4 0.5 fusion.21
  64.9 0.5 fusion.20
  65.3 87.1 %all-gather.5.cloned.1.call-done = bf16[1024,8192]{1,0:T(8,128)(2,1)} async-done(((bf16[1024,512]{1,0:T(8,128)(2,1)}), bf16[1024,8192]{1,0:T(8,128)(2,1)}) %all-gather.5.cloned.1.call-update) | async-done | bytes 16777232 | tf_op jit(solution)/shard_map/all_gather | solution.py:45
  152.4 16.3 %fusion.33 = (f32[1024]{0:T(1024)S(1)}, f32[1024,640]{0,1:T(8,128)S(1)}) fusion(bf16[1024,8192]{1,0:T(8,128)(2,1)} %all-gather.5.cloned.1.call-done, bf16[640,8192]{1,0:T(8,128)(2,1)} %param.9), kind=kOutput, calls=%fused_computation.52 | convolution fusion | flops 10738072576 | bytes 29888512 | tf_op jit(solution)/shard_map/dot_general | solution.py:49
  168.7 65.8 %pmax.7 = f32[1024]{0:T(1024)S(1)} all-reduce(f32[1024]{0:T(1024)S(1)} %get-tuple-element.10), channel_id=1, replica_groups=mesh['grp'=8,'vocab'=16] {'grp','vocab'}, use_global_device_ids=true, to_apply=%region_3.4 | all-reduce | flops 1024 | bytes 8192 | tf_op jit(solution)/shard_map/pmax | solution.py:54
  234.5 0.6 exponential_reduce_fusion
  235.2 63.1 %all-reduce = (f32[1024]{0:T(1024)S(1)}, f32[1024]{0:T(1024)S(1)}) all-reduce(f32[1024]{0:T(1024)S(1)} %get-tuple-element.4, f32[1024]{0:T(1024)S(1)} %get-tuple-element.3), channel_id=1, replica_groups=mesh['grp'=8,'vocab'=16] {'grp','vocab'}, use_global_device_ids=true, to_apply=%region_1.2 | all-reduce | flops 2048 | bytes 16384 | tf_op jit(solution)/shard_map/psum | solution.py:56
  298.2 0.6 multiply_reduce_fusion
  299.5 19.5 %convolution_convert_fusion = bf16[640,8192]{1,0:T(8,128)(2,1)} fusion(bf16[1024,8192]{1,0:T(8,128)(2,1)} %all-gather.5.cloned.1.call-done, f32[1024,640]{0,1:T(8,128)S(1)} %get-tuple-element.11, f32[1024]{0:T(1024)S(1)} %get-tuple-element.9, f32[1024]{0:T(1024)S(1)} %get-tuple-element.7, s32[1024]{0:T(1024)S(1)} %copy-done.3, s32[640]{0:T(1024)S(1)} %iota_add_fusion), kind=kOutput, calls=%fused_computation | convolution fusion | flops 10746593280 | bytes 29899264 | tf_op jit(solution)/shard_map/dot_general | solution.py:65
  (10 shorter events, 0.0 us)
Async XLA Ops:
  7.2 51.2 %all-gather.3.cloned.1.call-start = ((), (), s32[]{:S(2)}) async-start(), calls=%async_computation | async-start | bytes 1179648 | tf_op jit(solution)/shard_map/all_gather | solution.py:44
  7.9 144.5 %all-gather.5.cloned.1.call-start = ((), (), s32[]{:S(2)}) async-start(), calls=%async_computation.1 | async-start | bytes 17825792 | tf_op jit(solution)/shard_map/all_gather | solution.py:45
  65.3 169.2 %copy-start.3 = (s32[1024]{0:T(1024)S(1)}, s32[1024]{0:T(1024)}, u32[]{:S(2)}) copy-start(s32[1024]{0:T(1024)} %param.10) | copy-start | bytes 12292
  168.7 129.5 %copy-start = (s32[1024]{0:T(1024)S(1)}, s32[1024]{0:T(1024)}, u32[]{:S(2)}) copy-start(s32[1024]{0:T(1024)} %param.12) | copy-start | bytes 12292
  168.7 129.5 %copy-start.1 = (f32[1024]{0:T(1024)S(1)}, f32[1024]{0:T(1024)}, u32[]{:S(2)}) copy-start(f32[1024]{0:T(1024)} %param.11) | copy-start | bytes 12292
  298.2 20.8 %copy-start.2 = (f32[1024]{0:T(1024)}, f32[1024]{0:T(1024)S(1)}, u32[]{:S(2)}) copy-start(f32[1024]{0:T(1024)S(1)} %get-tuple-element.8) | copy-start | bytes 12292
Sparse Core Ops, SparseCore 0:
  10.3 48.0 all-gather.2
  60.1 92.3 all-gather.4
where the time goes:
time: 328 us; the launch traced here: 327 us
  waiting for transfers between devices  138 us (42%)
  blocking collectives  129 us (39%)
  matrix products  40.7 us (12%)
  between operations  15.9 us (5%)
    all_gather x1, waiting for transfers between devices, shards(): features = lax.all_gather(token_block, 'vocab', axis=1, tiled=True)  87.1 us
    pmax x1, blocking collectives, shards(): top = lax.pmax(jnp.max(logits, axis=1), ('grp', 'vocab'))  65.8 us
    psum x1, blocking collectives, shards(): total, target_logit = lax.psum((local_sum, picked), ('grp', 'vocab'))  63.1 us
    all_gather x1, waiting for transfers between devices, shards(): token_block = lax.all_gather(hidden, 'grp', axis=0, tiled=True)  50.5 us
    dot_general x1, matrix products, shards(): lax.dot_general(grads, features, (((0,), (0,)), ((), ())), preferred_elem...  19.5 us
    dot_general x1, matrix products, shards(): lax.dot_general(features, head_weight, (((1,), (1,)), ((), ())), preferre...  16.3 us
  transfers between devices with their start and end apart: 2, of which 2 were waited for; matrix products, arithmetic and copies ran while one was open for 2% of the time, Pallas kernels for 0%

commit v1 on v0

--- a/solution.py
+++ b/solution.py
@@ -41,7 +41,9 @@
 def shards(
     hidden, head_weight, targets, old_logprobs, loss_mask, beam_lengths, beam_group, rewards
 ):
-    token_block = lax.all_gather(hidden, "grp", axis=0, tiled=True)
+    token_block = jnp.concatenate(
+        lax.all_to_all(jnp.stack([hidden] * lax.axis_size("grp")), "grp", 0, 0), axis=0
+    )
     features = lax.all_gather(token_block, "vocab", axis=1, tiled=True)
     shard = head_weight.shape[0]
     offset = (lax.axis_index("grp") * lax.axis_size("vocab") + lax.axis_index("vocab")) * shard

time: 328 us -> 298 us (0.909)
  waiting for transfers between devices: 138 us -> 88.3 us
  blocking collectives: 129 us -> 153 us
    all_gather x1 -> x0, waiting for transfers between devices: 50.5 us -> none  [shards(): token_block = lax.all_gather(hidden, 'grp', axis=0, tiled=True)]
    all_to_all x0 -> x1, blocking collectives: none -> 23.9 us  [shards(): lax.all_to_all(jnp.stack([hidden] * lax.axis_size('grp')), 'grp', 0, 0)]
  transfers between devices with their start and end apart: 2 -> 1, of which waited for: 2 -> 1; matrix products, arithmetic and copies ran while one was open for 2% -> 1% of each run, Pallas kernels for 0% -> 0%
where the time goes in v1:
time: 298 us
  blocking collectives  153 us (51%)
  waiting for transfers between devices  88.3 us (30%)
  matrix products  38 us (13%)
  between operations  16 us (5%)
    all_gather x1, waiting for transfers between devices, shards(): features = lax.all_gather(token_block, 'vocab', axis=1, tiled=True)  88.3 us
    pmax x1, blocking collectives, shards(): top = lax.pmax(jnp.max(logits, axis=1), ('grp', 'vocab'))  65.8 us
    psum x1, blocking collectives, shards(): total, target_logit = lax.psum((local_sum, picked), ('grp', 'vocab'))  63.1 us
    all_to_all x1, blocking collectives, shards(): lax.all_to_all(jnp.stack([hidden] * lax.axis_size('grp')), 'grp', 0, 0)  23.9 us
    dot_general x1, matrix products, shards(): lax.dot_general(grads, features, (((0,), (0,)), ((), ())), preferred_elem...  19.6 us
    dot_general x1, matrix products, shards(): lax.dot_general(features, head_weight, (((1,), (1,)), ((), ())), preferre...  16.3 us
  transfers between devices with their start and end apart: 1, of which 1 were waited for; matrix products, arithmetic and copies ran while one was open for 1% of the time, Pallas kernels for 0%

profile of v1, /device:TPU:1, one launch (start us, length us, event | category | flops | bytes accessed | tf_op | source)
XLA Modules:
  0.0 298.0 jit_solution(2307766915366226348)
XLA Ops:
  7.2 0.0 all-gather.2.cloned.1.call-start
  7.3 1.0 stack.2
  8.2 23.9 %all_to_all.5 = bf16[8,128,512]{2,1,0:T(8,128)(2,1)} all-to-all(bf16[8,128,512]{2,1,0:T(8,128)(2,1)S(1)} %stack.2), channel_id=1, replica_groups=mesh['grp'=8,'vocab'=16] {'grp'}, dimensions={0} | all-to-all | bytes 2097152 | tf_op jit(solution)/shard_map/all_to_all | solution.py:45
  32.1 0.0 all-gather.2.cloned.1.call-update
  32.2 0.1 copy.13
  32.3 0.2 reduce-window.8
  32.5 0.1 reduce
  32.6 0.2 fusion.15
  32.8 0.2 fusion.13
  33.0 0.3 fusion.12
  33.3 0.2 fusion.17
  33.5 0.3 convert_reduce_fusion
  33.8 0.4 fusion.19
  34.2 0.5 fusion.21
  34.6 0.5 fusion.20
  35.1 88.3 %all-gather.2.cloned.1.call-done = bf16[1024,8192]{1,0:T(8,128)(2,1)} async-done(((bf16[1024,512]{1,0:T(8,128)(2,1)}), bf16[1024,8192]{1,0:T(8,128)(2,1)}) %all-gather.2.cloned.1.call-update) | async-done | bytes 16777232 | tf_op jit(solution)/shard_map/all_gather | solution.py:47
  123.4 16.3 %fusion.33 = (f32[1024]{0:T(1024)S(1)}, f32[1024,640]{0,1:T(8,128)S(1)}) fusion(bf16[1024,8192]{1,0:T(8,128)(2,1)} %all-gather.2.cloned.1.call-done, bf16[640,8192]{1,0:T(8,128)(2,1)} %param.9), kind=kOutput, calls=%fused_computation.52 | convolution fusion | flops 10738072576 | bytes 29888512 | tf_op jit(solution)/shard_map/dot_general | solution.py:51
  139.7 0.0 copy-start.1
  139.7 65.8 %pmax.7 = f32[1024]{0:T(1024)S(1)} all-reduce(f32[1024]{0:T(1024)S(1)} %get-tuple-element.10), channel_id=1, replica_groups=mesh['grp'=8,'vocab'=16] {'grp','vocab'}, use_global_device_ids=true, to_apply=%region_3.4 | all-reduce | flops 1024 | bytes 8192 | tf_op jit(solution)/shard_map/pmax | solution.py:56
  205.5 0.6 exponential_reduce_fusion
  206.2 63.1 %all-reduce = (f32[1024]{0:T(1024)S(1)}, f32[1024]{0:T(1024)S(1)}) all-reduce(f32[1024]{0:T(1024)S(1)} %get-tuple-element.4, f32[1024]{0:T(1024)S(1)} %get-tuple-element.3), channel_id=1, replica_groups=mesh['grp'=8,'vocab'=16] {'grp','vocab'}, use_global_device_ids=true, to_apply=%region_1.2 | all-reduce | flops 2048 | bytes 16384 | tf_op jit(solution)/shard_map/psum | solution.py:58
  269.2 0.0 copy-start.2
  269.2 0.6 multiply_reduce_fusion
  270.5 19.6 %convolution_convert_fusion = bf16[640,8192]{1,0:T(8,128)(2,1)} fusion(bf16[1024,8192]{1,0:T(8,128)(2,1)} %all-gather.2.cloned.1.call-done, f32[1024,640]{0,1:T(8,128)S(1)} %get-tuple-element.11, f32[1024]{0:T(1024)S(1)} %get-tuple-element.9, f32[1024]{0:T(1024)S(1)} %get-tuple-element.7, s32[1024]{0:T(1024)S(1)} %copy-done.3, s32[640]{0:T(1024)S(1)} %iota_add_fusion), kind=kOutput, calls=%fused_computation | convolution fusion | flops 10746593280 | bytes 29899264 | tf_op jit(solution)/shard_map/dot_general | solution.py:67
  (15 shorter events, 0.0 us)
Async XLA Ops:
  7.2 25.0 %copy-start = (s32[1024]{0:T(1024)S(1)}, s32[1024]{0:T(1024)}, u32[]{:S(2)}) copy-start(s32[1024]{0:T(1024)} %param.12) | copy-start | bytes 12292
  7.2 25.0 %copy-start.4 = (s32[128]{0:T(128)S(1)}, s32[128]{0:T(128)}, u32[]{:S(2)}) copy-start(s32[128]{0:T(128)} %param.13) | copy-start | bytes 1540
  7.2 25.4 %copy-start.6 = (s32[128]{0:T(128)S(1)}, s32[128]{0:T(128)}, u32[]{:S(2)}) copy-start(s32[128]{0:T(128)} %param.14) | copy-start | bytes 1540
  7.2 25.4 %copy-start.5 = (f32[128]{0:T(128)S(1)}, f32[128]{0:T(128)}, u32[]{:S(2)}) copy-start(f32[128]{0:T(128)} %param.15) | copy-start | bytes 1540
  7.2 116.2 %all-gather.2.cloned.1.call-start = ((), (), s32[]{:S(2)}) async-start(), calls=%async_computation.1 | async-start | bytes 17825792 | tf_op jit(solution)/shard_map/all_gather | solution.py:47
  35.1 170.4 %copy-start.3 = (s32[1024]{0:T(1024)S(1)}, s32[1024]{0:T(1024)}, u32[]{:S(2)}) copy-start(s32[1024]{0:T(1024)} %param.10) | copy-start | bytes 12292
  139.7 129.5 %copy-start.1 = (f32[1024]{0:T(1024)S(1)}, f32[1024]{0:T(1024)}, u32[]{:S(2)}) copy-start(f32[1024]{0:T(1024)} %param.11) | copy-start | bytes 12292
  269.2 20.8 %copy-start.2 = (f32[1024]{0:T(1024)}, f32[1024]{0:T(1024)S(1)}, u32[]{:S(2)}) copy-start(f32[1024]{0:T(1024)S(1)} %get-tuple-element.8) | copy-start | bytes 12292
Sparse Core Ops, SparseCore 0:
  32.3 91.1 all-gather.1
